TPU v7x, 32 devices: a whole 2x2x4 slice. The times are simulated.
32 devices in a mesh: grid: 8 (over z, y), band: 4 (over x, core).
Axes of the slice: x: 2, y: 2, z: 4, core: 2. Of those that a mesh axis runs over, the one named last changes fastest.
Arguments:
- orbitals: float32 [2048, 512], P('grid', 'band'), may hold values from -30 to 30
- potential: float32 [2048], P('grid'), may hold values from -1 to 1
- fitted: bfloat16 [512, 2048], P('band', 'grid'), may hold values from -6 to 6
- points: int32 [512], P('grid'), may hold values from -1 to 255, as said below
Outputs:
- updated: float32 [2048, 512], P('grid', 'band')
Inputs may be any that keep to these rules, and one draw needn't show every extreme that they name: Each block of 64 slots of one index of grid holds distinct grid points in its first slots and -1 in the rest; the numbers of filled slots of blocks 2i and 2i + 1 sum to 64, so that 256 slots are filled in all, and some block is full.
All inputs are finite; a program needn't handle non-finite values.
Results may differ from a plain program's by a relative error of at most 0.024.
Values may be sent and summed in bfloat16 or wider, within the bound.
No kernel may reach another device: no remote copies, remote signals or barrier semaphores. Data moves between devices by JAX's collectives and lax.ppermute only.
A program may use at most 64 MiB of HBM per device.

v0:
```python
import jax
import jax.numpy as jnp
from jax import lax
from jax.sharding import PartitionSpec as P

ITERS = 2


def body(orbitals, potential, fitted, points):
    rows = orbitals.shape[0]
    block_width = orbitals.shape[1]
    nbands = lax.axis_size("band")
    ngroups = lax.axis_size("grid")
    total_orbitals = block_width * nbands
    valid_mask = points >= 0
    safe_idx = jnp.where(valid_mask, points, 0)
    psi = orbitals
    for step in range(ITERS):
        orbital_block = psi.astype(jnp.bfloat16)
        selected_points = jnp.where(
            valid_mask[:, None], orbital_block[safe_idx], jnp.zeros((), jnp.bfloat16)
        )
        collocation_matrix = lax.all_gather(selected_points, "grid", axis=0, tiled=True)
        product = lax.dot_general(
            collocation_matrix,
            orbital_block,
            (((1,), (1,)), ((), ())),
            preferred_element_type=jnp.float32,
        )
        proj = lax.psum_scatter(
            (product / total_orbitals).astype(jnp.bfloat16), "band", scatter_dimension=0, tiled=True
        ).astype(jnp.float32)
        tile_blocks = (fitted.astype(jnp.float32) * proj).astype(jnp.bfloat16)
        orbitals_at_slots = lax.all_to_all(
            collocation_matrix, "band", split_axis=0, concat_axis=1, tiled=True
        )
        partial_value = lax.dot_general(
            tile_blocks,
            orbitals_at_slots,
            (((0,), (0,)), ((), ())),
            preferred_element_type=jnp.float32,
        )
        applied = lax.psum_scatter(
            partial_value.astype(jnp.bfloat16), "band", scatter_dimension=1, tiled=True
        ).astype(jnp.float32)
        fresh = psi - 0.25 * (potential[:, None] * psi - applied)
        squares = lax.psum(jnp.sum(fresh * fresh, axis=0), "grid")
        psi = fresh * lax.rsqrt(squares / (rows * ngroups) + 1e-06)
    return psi


def solution(mesh):
    in_specs = (P("grid", "band"), P("grid"), P("band", "grid"), P("grid"))
    out_specs = P("grid", "band")
    return jax.shard_map(body, mesh=mesh, in_specs=in_specs, out_specs=out_specs, check_vma=False)
```

profile of v0, /device:TPU:0, one launch (start us, length us, event | category | flops | bytes accessed | tf_op | source)
XLA Modules:
  0.0 209.6 jit_solution(11900437040815080563)
XLA Ops:
  6.5 0.0 copy-start.3
  6.5 0.0 reduce-scatter.9.cloned.1.call-start
  6.5 0.7 compare_select_fusion
  7.3 0.0 copy-done.3
  7.3 0.9 convert_element_type.41
  8.2 0.6 gather_fusion
  8.8 0.1 broadcast_select_fusion.1
  8.9 32.3 %all_gather.6 = bf16[512,128]{1,0:T(8,128)(2,1)S(1)} all-gather(bf16[64,128]{1,0:T(8,128)(2,1)S(1)} %broadcast_select_fusion.1), channel_id=1, replica_groups=mesh['grid'=8,'band'=4] {'grid'}, dimensions={0}, use_global_device_ids=true | all-gather | bytes 147456 | tf_op jit(solution)/shard_map/all_gather | solution.py:23
  41.2 0.9 fusion
  42.1 0.0 reduce-scatter.9.cloned.1.call-update
  42.2 0.0 reduce-scatter.13.cloned.1.call-start
  42.2 0.1 copy.7
  42.4 0.0 copy-start.1
  42.4 7.3 %all_to_all.38 = bf16[4,128,128]{1,2,0:T(8,128)(2,1)S(1)} all-to-all(bf16[4,128,128]{1,2,0:T(8,128)(2,1)S(1)} %copy.7), channel_id=1, replica_groups=mesh['grid'=8,'band'=4] {'band'}, dimensions={0} | all-to-all | bytes 262144 | tf_op jit(solution)/shard_map/all_to_all | solution.py:34
  49.7 13.6 %reduce-scatter.9.cloned.1.call-done = bf16[128,256]{1,0:T(8,128)(2,1)} async-done(((bf16[512,256]{1,0:T(8,128)(2,1)}), bf16[128,256]{1,0:T(8,128)(2,1)}) %reduce-scatter.9.cloned.1.call-update) | async-done | bytes 65552 | tf_op jit(solution)/shard_map/reduce_scatter | solution.py:30
  63.3 0.0 copy-done.1
  63.3 1.1 convolution_convert_fusion.1
  64.4 0.8 copy.9
  65.2 0.0 reduce-scatter.13.cloned.1.call-update
  65.2 0.0 copy-start
  65.3 0.0 reduce-scatter.11.cloned.1.call-start
  65.3 20.6 %reduce-scatter.13.cloned.1.call-done = bf16[128,256]{1,0:T(8,128)(2,1)} async-done(((bf16[512,256]{1,0:T(8,128)(2,1)}), bf16[128,256]{1,0:T(8,128)(2,1)}) %reduce-scatter.13.cloned.1.call-update) | async-done | bytes 65552
  85.9 0.0 copy-start.2
  85.9 1.0 copy.10
  86.9 0.0 copy-done
  86.9 0.0 copy-done.2
  86.9 0.1 multiply_reduce_fusion.1
  87.0 21.4 %psum.14 = f32[128]{0:T(128)S(1)} all-reduce(f32[128]{0:T(128)S(1)} %multiply_reduce_fusion.1), channel_id=1, replica_groups=mesh['grid'=8,'band'=4] {'grid'}, use_global_device_ids=true, to_apply=%region_3.4 | all-reduce | flops 128 | bytes 1024 | tf_op jit(solution)/shard_map/psum | solution.py:47
  108.4 0.1 multiply_convert_fusion
  108.5 0.6 gather_fusion.1
  109.2 0.1 broadcast_select_fusion
  109.3 30.5 %all_gather.7 = bf16[512,128]{1,0:T(8,128)(2,1)S(1)} all-gather(bf16[64,128]{1,0:T(8,128)(2,1)S(1)} %broadcast_select_fusion), channel_id=1, replica_groups=mesh['grid'=8,'band'=4] {'grid'}, dimensions={0}, use_global_device_ids=true | all-gather | bytes 147456 | tf_op jit(solution)/shard_map/all_gather | solution.py:23
  139.8 0.9 fusion.1
  140.7 0.0 reduce-scatter.11.cloned.1.call-update
  140.7 0.0 reduce-scatter.15.cloned.1.call-start
  140.8 0.1 copy.8
  140.9 7.0 %all_to_all.39 = bf16[4,128,128]{1,2,0:T(8,128)(2,1)S(1)} all-to-all(bf16[4,128,128]{1,2,0:T(8,128)(2,1)S(1)} %copy.8), channel_id=1, replica_groups=mesh['grid'=8,'band'=4] {'band'}, dimensions={0} | all-to-all | bytes 262144 | tf_op jit(solution)/shard_map/all_to_all | solution.py:34
  147.9 9.3 %reduce-scatter.11.cloned.1.call-done = bf16[128,256]{1,0:T(8,128)(2,1)} async-done(((bf16[512,256]{1,0:T(8,128)(2,1)}), bf16[128,256]{1,0:T(8,128)(2,1)}) %reduce-scatter.11.cloned.1.call-update) | async-done | bytes 65552 | tf_op jit(solution)/shard_map/reduce_scatter | solution.py:30
  157.3 1.1 convolution_convert_fusion
  158.3 0.8 copy.11
  159.2 0.0 reduce-scatter.15.cloned.1.call-update
  159.2 20.6 %reduce-scatter.15.cloned.1.call-done = bf16[128,256]{1,0:T(8,128)(2,1)} async-done(((bf16[512,256]{1,0:T(8,128)(2,1)}), bf16[128,256]{1,0:T(8,128)(2,1)}) %reduce-scatter.15.cloned.1.call-update) | async-done | bytes 65552
  179.8 0.9 copy.12
  180.7 0.1 multiply_reduce_fusion
  180.9 21.4 %psum.15 = f32[128]{0:T(128)S(1)} all-reduce(f32[128]{0:T(128)S(1)} %multiply_reduce_fusion), channel_id=1, replica_groups=mesh['grid'=8,'band'=4] {'grid'}, use_global_device_ids=true, to_apply=%region_7.8 | all-reduce | flops 128 | bytes 1024 | tf_op jit(solution)/shard_map/psum | solution.py:47
  202.3 0.8 broadcast_multiply_fusion
  (4 shorter events, 0.0 us)
Async XLA Ops:
  6.5 0.7 copy-start.3
  6.5 56.7 %reduce-scatter.9.cloned.1.call-start = ((), (), s32[]{:S(2)}) async-start(), calls=%async_computation.6 | async-start | bytes 327680 | tf_op jit(solution)/shard_map/reduce_scatter | solution.py:30
  42.2 43.8 %reduce-scatter.13.cloned.1.call-start = ((), (), s32[]{:S(2)}) async-start(), calls=%async_computation.8 | async-start | bytes 327680
  42.4 20.9 %copy-start.1 = (bf16[128,256]{1,0:T(8,128)(2,1)S(1)}, bf16[128,256]{1,0:T(8,128)(2,1)}, u32[]{:S(2)}) copy-start(bf16[128,256]{1,0:T(8,128)(2,1)} %param.6) | copy-start | bytes 196612
  65.2 21.7 %copy-start = (f32[256,128]{1,0:T(8,128)S(1)}, f32[256,128]{1,0:T(8,128)}, u32[]{:S(2)}) copy-start(f32[256,128]{1,0:T(8,128)} %param.4) | copy-start | bytes 393220
  65.3 92.0 %reduce-scatter.11.cloned.1.call-start = ((), (), s32[]{:S(2)}) async-start(), calls=%async_computation.7 | async-start | bytes 327680 | tf_op jit(solution)/shard_map/reduce_scatter | solution.py:30
  85.9 1.0 copy-start.2
  140.7 39.1 %reduce-scatter.15.cloned.1.call-start = ((), (), s32[]{:S(2)}) async-start(), calls=%async_computation.9 | async-start | bytes 327680
Sparse Core Ops, SparseCore 0:
  42.3 20.9 reduce-scatter.8
  65.9 19.9 reduce-scatter.12
  140.8 16.3 reduce-scatter.10
  159.7 20.0 reduce-scatter.14
where the time goes:
time: 210 us
  blocking collectives  120 us (57%)
  waiting for transfers between devices  64.2 us (31%)
  between operations  13.2 us (6%)
  local copies, waits for them, and re-layouts  5.13 us (2%)
  matrix products  4.03 us (2%)
  other arithmetic  2.98 us (1%)
    all_gather x2, blocking collectives, body(): lax.all_gather(selected_points, 'grid', axis=0, tiled=True)  62.8 us
    psum x2, blocking collectives, body(): squares = lax.psum(jnp.sum(fresh * fresh, axis=0), 'grid')  42.8 us
    unnamed x6, waiting for transfers between devices  41.3 us
    reduce_scatter x2, waiting for transfers between devices, body(): lax.psum_scatter((product / total_orbitals).astype(jnp.bfloat16), 'band',...  22.9 us
    all_to_all x2, blocking collectives, body(): lax.all_to_all(collocation_matrix, 'band', split_axis=0, concat_axis=1, t...  14.3 us
  transfers between devices with their start and end apart: 4, of which 4 were waited for; matrix products, arithmetic and copies ran while one was open for 0% of the time, Pallas kernels for 0%

commit v1 on v0

--- a/solution.py
+++ b/solution.py
@@ -20,7 +20,31 @@
         selected_points = jnp.where(
             valid_mask[:, None], orbital_block[safe_idx], jnp.zeros((), jnp.bfloat16)
         )
-        collocation_matrix = lax.all_gather(selected_points, "grid", axis=0, tiled=True)
+        devices, position, width = (
+            lax.axis_size("grid"),
+            lax.axis_index("grid"),
+            selected_points.shape[0],
+        )
+        right = [(i, (i + 1) % devices) for i in range(devices)]
+        left = [(i, (i - 1) % devices) for i in range(devices)]
+        out = jnp.zeros(
+            (*selected_points.shape[:0], devices * width, *selected_points.shape[0 + 1 :]),
+            selected_points.dtype,
+        )
+        out = lax.dynamic_update_slice_in_dim(out, selected_points, position * width, axis=0)
+        from_left = from_right = selected_points
+        half = devices // 2
+        for step_2 in range(1, half + 1):
+            from_left = lax.ppermute(from_left, "grid", right)
+            out = lax.dynamic_update_slice_in_dim(
+                out, from_left, (position - step_2) % devices * width, axis=0
+            )
+            if step_2 < devices - half:
+                from_right = lax.ppermute(from_right, "grid", left)
+                out = lax.dynamic_update_slice_in_dim(
+                    out, from_right, (position + step_2) % devices * width, axis=0
+                )
+        collocation_matrix = out
         product = lax.dot_general(
             collocation_matrix,
             orbital_block,

time: 210 us -> 197 us (0.938)
  blocking collectives: 120 us -> 57.1 us
  starting transfers between devices: 0.13 us -> 30.2 us
  waiting for transfers between devices: 64.2 us -> 83.4 us
    all_gather x2 -> x0, blocking collectives: 62.8 us -> none  [body(): lax.all_gather(selected_points, 'grid', axis=0, tiled=True)]
    ppermute x0 -> x14, starting transfers between devices: none -> 30.1 us  [the longest x6 27 us: body(): from_right = lax.ppermute(from_right, 'grid', left)]
    ppermute x0 -> x14, waiting for transfers between devices: none -> 22.7 us  [the longest x8 22.7 us: body(): from_left = lax.ppermute(from_left, 'grid', right)]
    reduce_scatter x2, waiting for transfers between devices: 22.9 us -> 19.4 us  [body(): lax.psum_scatter((product / total_orbitals).astype(jnp.bfloat16), 'band',...]
  transfers between devices with their start and end apart: 4 -> 18, of which waited for: 4 -> 12; matrix products, arithmetic and copies ran while one was open for 0% -> 0% of each run, Pallas kernels for 0% -> 0%
where the time goes in v1:
time: 197 us; the launch traced here: 196 us
  waiting for transfers between devices  83.4 us (42%)
  blocking collectives  57.1 us (29%)
  starting transfers between devices  30.2 us (15%)
  between operations  13.3 us (7%)
  local copies, waits for them, and re-layouts  5.94 us (3%)
  matrix products  4.01 us (2%)
  other arithmetic  2.29 us (1%)
    psum x2, blocking collectives, body(): squares = lax.psum(jnp.sum(fresh * fresh, axis=0), 'grid')  42.7 us
    unnamed x6, waiting for transfers between devices  41.3 us
    ppermute x6, starting transfers between devices, body(): from_right = lax.ppermute(from_right, 'grid', left)  27 us
    ppermute x8, waiting for transfers between devices, body(): from_left = lax.ppermute(from_left, 'grid', right)  22.7 us
    reduce_scatter x2, waiting for transfers between devices, body(): lax.psum_scatter((product / total_orbitals).astype(jnp.bfloat16), 'band',...  19.4 us
    all_to_all x2, blocking collectives, body(): lax.all_to_all(collocation_matrix, 'band', split_axis=0, concat_axis=1, t...  14.4 us
    unnamed x12, local copies, waits for them, and re-layouts  4.24 us
  transfers between devices with their start and end apart: 18, of which 12 were waited for; matrix products, arithmetic and copies ran while one was open for 0% of the time, Pallas kernels for 0%

profile of v1, /device:TPU:0, one launch (start us, length us, event | category | flops | bytes accessed | tf_op | source)
XLA Modules:
  0.0 196.2 jit_solution(9249835438079931413)
XLA Ops:
  6.5 0.7 copy-done.3
  7.2 0.9 convert_element_type.41
  8.1 0.6 gather_fusion
  8.8 0.1 constant_dynamic-update-slice_fusion.15
  8.9 3.0 %collective-permute-start = (bf16[64,128]{1,0:T(8,128)(2,1)S(1)}, bf16[64,128]{1,0:T(8,128)(2,1)S(1)}, u32[]{:S(2)}, u32[]{:S(2)}) collective-permute-start(bf16[64,128]{1,0:T(8,128)(2,1)S(1)} %get-tuple-element.8), channel_id=1, source_target_pairs={{0,4},{4,8},{8,12},{12,16},{16,20},{20,24},{24,28},{28,0},{1,5},{5... | collective-permute-start | bytes 49160 | tf_op jit(solution)/shard_map/ppermute | solution.py:38
  11.9 3.1 %collective-permute-start.1 = (bf16[64,128]{1,0:T(8,128)(2,1)S(1)}, bf16[64,128]{1,0:T(8,128)(2,1)S(1)}, u32[]{:S(2)}, u32[]{:S(2)}) collective-permute-start(bf16[64,128]{1,0:T(8,128)(2,1)S(1)} %get-tuple-element.8), channel_id=1, source_target_pairs={{0,28},{4,0},{8,4},{12,8},{16,12},{20,16},{24,20},{28,24},{1,29},{... | collective-permute-start | bytes 49160 | tf_op jit(solution)/shard_map/ppermute | solution.py:43
  15.0 1.7 collective-permute-done
  16.7 0.0 collective-permute-start.2
  16.7 0.0 collective-permute-done.1
  16.7 4.8 %collective-permute-start.3 = (bf16[64,128]{1,0:T(8,128)(2,1)S(1)}, bf16[64,128]{1,0:T(8,128)(2,1)S(1)}, u32[]{:S(2)}, u32[]{:S(2)}) collective-permute-start(bf16[64,128]{1,0:T(8,128)(2,1)S(1)} %collective-permute-done.1), channel_id=1, source_target_pairs={{0,28},{4,0},{8,4},{12,8},{16,12},{20,16},{24,20},{28,24},{1,29},{... | collective-permute-start | bytes 49160 | tf_op jit(solution)/shard_map/ppermute | solution.py:43
  21.5 1.6 collective-permute-done.2
  23.1 0.0 collective-permute-start.4
  23.1 0.0 collective-permute-done.3
  23.1 4.8 %collective-permute-start.5 = (bf16[64,128]{1,0:T(8,128)(2,1)S(1)}, bf16[64,128]{1,0:T(8,128)(2,1)S(1)}, u32[]{:S(2)}, u32[]{:S(2)}) collective-permute-start(bf16[64,128]{1,0:T(8,128)(2,1)S(1)} %collective-permute-done.3), channel_id=1, source_target_pairs={{0,28},{4,0},{8,4},{12,8},{16,12},{20,16},{24,20},{28,24},{1,29},{... | collective-permute-start | bytes 49160 | tf_op jit(solution)/shard_map/ppermute | solution.py:43
  27.9 1.6 collective-permute-done.4
  29.5 0.0 collective-permute-start.6
  29.5 0.0 collective-permute-done.5
  29.6 6.4 %collective-permute-done.6 = bf16[64,128]{1,0:T(8,128)(2,1)S(1)} collective-permute-done((bf16[64,128]{1,0:T(8,128)(2,1)S(1)}, bf16[64,128]{1,0:T(8,128)(2,1)S(1)}, u32[]{:S(2)}, u32[]{:S(2)}) %collective-permute-start.6) | collective-permute-done | bytes 16416 | tf_op jit(solution)/shard_map/ppermute | solution.py:38
  36.0 0.9 fusion
  36.9 0.0 reduce-scatter.9.cloned.1.call-update
  36.9 0.0 reduce-scatter.13.cloned.1.call-start
  37.0 7.3 %all_to_all.38 = bf16[4,128,128]{2,1,0:T(8,128)(2,1)S(1)} all-to-all(bf16[4,128,128]{2,1,0:T(8,128)(2,1)S(1)} %bitcast.17), channel_id=1, replica_groups=mesh['grid'=8,'band'=4] {'band'}, dimensions={0} | all-to-all | bytes 262144 | tf_op jit(solution)/shard_map/all_to_all | solution.py:58
  44.3 0.1 copy.7
  44.5 10.1 %reduce-scatter.9.cloned.1.call-done = bf16[128,256]{1,0:T(8,128)(2,1)} async-done(((bf16[512,256]{1,0:T(8,128)(2,1)}), bf16[128,256]{1,0:T(8,128)(2,1)}) %reduce-scatter.9.cloned.1.call-update) | async-done | bytes 65552 | tf_op jit(solution)/shard_map/reduce_scatter | solution.py:54
  54.6 1.1 convolution_convert_fusion.1
  55.6 0.8 copy.9
  56.5 0.0 reduce-scatter.13.cloned.1.call-update
  56.5 0.0 copy-start
  56.5 0.0 reduce-scatter.11.cloned.1.call-start
  56.6 20.7 %reduce-scatter.13.cloned.1.call-done = bf16[128,256]{1,0:T(8,128)(2,1)} async-done(((bf16[512,256]{1,0:T(8,128)(2,1)}), bf16[128,256]{1,0:T(8,128)(2,1)}) %reduce-scatter.13.cloned.1.call-update) | async-done | bytes 65552
  77.2 1.0 copy.10
  78.2 0.1 multiply_reduce_fusion.1
  78.3 21.4 %psum.14 = f32[128]{0:T(128)S(1)} all-reduce(f32[128]{0:T(128)S(1)} %multiply_reduce_fusion.1), channel_id=1, replica_groups=mesh['grid'=8,'band'=4] {'grid'}, use_global_device_ids=true, to_apply=%region_3.4 | all-reduce | flops 128 | bytes 1024 | tf_op jit(solution)/shard_map/psum | solution.py:71
  99.7 0.1 multiply_convert_fusion
  99.8 0.6 gather_fusion.1
  100.5 0.1 constant_dynamic-update-slice_fusion.7
  100.6 0.1 collective-permute-start.7
  100.6 4.7 %collective-permute-start.8 = (bf16[64,128]{1,0:T(8,128)(2,1)S(1)}, bf16[64,128]{1,0:T(8,128)(2,1)S(1)}, u32[]{:S(2)}, u32[]{:S(2)}) collective-permute-start(bf16[64,128]{1,0:T(8,128)(2,1)S(1)} %get-tuple-element.6), channel_id=1, source_target_pairs={{0,28},{4,0},{8,4},{12,8},{16,12},{20,16},{24,20},{28,24},{1,29},{... | collective-permute-start | bytes 49160 | tf_op jit(solution)/shard_map/ppermute | solution.py:43
  105.3 1.7 collective-permute-done.7
  107.1 0.0 collective-permute-start.9
  107.1 0.0 collective-permute-done.8
  107.1 4.8 %collective-permute-start.10 = (bf16[64,128]{1,0:T(8,128)(2,1)S(1)}, bf16[64,128]{1,0:T(8,128)(2,1)S(1)}, u32[]{:S(2)}, u32[]{:S(2)}) collective-permute-start(bf16[64,128]{1,0:T(8,128)(2,1)S(1)} %collective-permute-done.8), channel_id=1, source_target_pairs={{0,28},{4,0},{8,4},{12,8},{16,12},{20,16},{24,20},{28,24},{1,29},{... | collective-permute-start | bytes 49160 | tf_op jit(solution)/shard_map/ppermute | solution.py:43
  111.9 1.6 collective-permute-done.9
  113.5 0.0 collective-permute-start.11
  113.5 0.0 collective-permute-done.10
  113.5 4.8 %collective-permute-start.12 = (bf16[64,128]{1,0:T(8,128)(2,1)S(1)}, bf16[64,128]{1,0:T(8,128)(2,1)S(1)}, u32[]{:S(2)}, u32[]{:S(2)}) collective-permute-start(bf16[64,128]{1,0:T(8,128)(2,1)S(1)} %collective-permute-done.10), channel_id=1, source_target_pairs={{0,28},{4,0},{8,4},{12,8},{16,12},{20,16},{24,20},{28,24},{1,29},{... | collective-permute-start | bytes 49160 | tf_op jit(solution)/shard_map/ppermute | solution.py:43
  118.3 1.6 collective-permute-done.11
  119.9 0.0 collective-permute-start.13
  119.9 0.0 collective-permute-done.12
  120.0 6.4 %collective-permute-done.13 = bf16[64,128]{1,0:T(8,128)(2,1)S(1)} collective-permute-done((bf16[64,128]{1,0:T(8,128)(2,1)S(1)}, bf16[64,128]{1,0:T(8,128)(2,1)S(1)}, u32[]{:S(2)}, u32[]{:S(2)}) %collective-permute-start.13) | collective-permute-done | bytes 16416 | tf_op jit(solution)/shard_map/ppermute | solution.py:38
  126.4 0.9 fusion.1
  127.3 0.0 reduce-scatter.11.cloned.1.call-update
  127.3 0.0 reduce-scatter.15.cloned.1.call-start
  127.4 7.0 %all_to_all.39 = bf16[4,128,128]{2,1,0:T(8,128)(2,1)S(1)} all-to-all(bf16[4,128,128]{2,1,0:T(8,128)(2,1)S(1)} %bitcast.16), channel_id=1, replica_groups=mesh['grid'=8,'band'=4] {'band'}, dimensions={0} | all-to-all | bytes 262144 | tf_op jit(solution)/shard_map/all_to_all | solution.py:58
  134.4 0.1 copy.8
  134.5 9.3 %reduce-scatter.11.cloned.1.call-done = bf16[128,256]{1,0:T(8,128)(2,1)} async-done(((bf16[512,256]{1,0:T(8,128)(2,1)}), bf16[128,256]{1,0:T(8,128)(2,1)}) %reduce-scatter.11.cloned.1.call-update) | async-done | bytes 65552 | tf_op jit(solution)/shard_map/reduce_scatter | solution.py:54
  143.8 1.1 convolution_convert_fusion
  144.9 0.8 copy.11
  145.8 0.0 reduce-scatter.15.cloned.1.call-update
  145.8 20.6 %reduce-scatter.15.cloned.1.call-done = bf16[128,256]{1,0:T(8,128)(2,1)} async-done(((bf16[512,256]{1,0:T(8,128)(2,1)}), bf16[128,256]{1,0:T(8,128)(2,1)}) %reduce-scatter.15.cloned.1.call-update) | async-done | bytes 65552
  166.4 0.9 copy.12
  167.3 0.1 multiply_reduce_fusion
  167.5 21.3 %psum.15 = f32[128]{0:T(128)S(1)} all-reduce(f32[128]{0:T(128)S(1)} %multiply_reduce_fusion), channel_id=1, replica_groups=mesh['grid'=8,'band'=4] {'grid'}, use_global_device_ids=true, to_apply=%region_7.8 | all-reduce | flops 128 | bytes 1024 | tf_op jit(solution)/shard_map/psum | solution.py:71
  188.8 0.8 broadcast_multiply_fusion
  (28 shorter events, 0.2 us)
Async XLA Ops:
  6.5 0.7 copy-start.3
  6.5 48.0 %reduce-scatter.9.cloned.1.call-start = ((), (), s32[]{:S(2)}) async-start(), calls=%async_computation.6 | async-start | bytes 327680 | tf_op jit(solution)/shard_map/reduce_scatter | solution.py:54
  8.9 7.8 %collective-permute-start = (bf16[64,128]{1,0:T(8,128)(2,1)S(1)}, bf16[64,128]{1,0:T(8,128)(2,1)S(1)}, u32[]{:S(2)}, u32[]{:S(2)}) collective-permute-start(bf16[64,128]{1,0:T(8,128)(2,1)S(1)} %get-tuple-element.8), channel_id=1, source_target_pairs={{0,4},{4,8},{8,12},{12,16},{16,20},{20,24},{24,28},{28,0},{1,5},{5... | collective-permute-start | bytes 49160 | tf_op jit(solution)/shard_map/ppermute | solution.py:38
  11.9 4.8 %collective-permute-start.1 = (bf16[64,128]{1,0:T(8,128)(2,1)S(1)}, bf16[64,128]{1,0:T(8,128)(2,1)S(1)}, u32[]{:S(2)}, u32[]{:S(2)}) collective-permute-start(bf16[64,128]{1,0:T(8,128)(2,1)S(1)} %get-tuple-element.8), channel_id=1, source_target_pairs={{0,28},{4,0},{8,4},{12,8},{16,12},{20,16},{24,20},{28,24},{1,29},{... | collective-permute-start | bytes 49160 | tf_op jit(solution)/shard_map/ppermute | solution.py:43
  16.7 6.4 %collective-permute-start.2 = (bf16[64,128]{1,0:T(8,128)(2,1)S(1)}, bf16[64,128]{1,0:T(8,128)(2,1)S(1)}, u32[]{:S(2)}, u32[]{:S(2)}) collective-permute-start(bf16[64,128]{1,0:T(8,128)(2,1)S(1)} %collective-permute-done), channel_id=1, source_target_pairs={{0,4},{4,8},{8,12},{12,16},{16,20},{20,24},{24,28},{28,0},{1,5},{5... | collective-permute-start | bytes 49160 | tf_op jit(solution)/shard_map/ppermute | solution.py:38
  16.7 6.4 %collective-permute-start.3 = (bf16[64,128]{1,0:T(8,128)(2,1)S(1)}, bf16[64,128]{1,0:T(8,128)(2,1)S(1)}, u32[]{:S(2)}, u32[]{:S(2)}) collective-permute-start(bf16[64,128]{1,0:T(8,128)(2,1)S(1)} %collective-permute-done.1), channel_id=1, source_target_pairs={{0,28},{4,0},{8,4},{12,8},{16,12},{20,16},{24,20},{28,24},{1,29},{... | collective-permute-start | bytes 49160 | tf_op jit(solution)/shard_map/ppermute | solution.py:43
  23.1 6.4 %collective-permute-start.4 = (bf16[64,128]{1,0:T(8,128)(2,1)S(1)}, bf16[64,128]{1,0:T(8,128)(2,1)S(1)}, u32[]{:S(2)}, u32[]{:S(2)}) collective-permute-start(bf16[64,128]{1,0:T(8,128)(2,1)S(1)} %collective-permute-done.2), channel_id=1, source_target_pairs={{0,4},{4,8},{8,12},{12,16},{16,20},{20,24},{24,28},{28,0},{1,5},{5... | collective-permute-start | bytes 49160 | tf_op jit(solution)/shard_map/ppermute | solution.py:38
  23.1 6.4 %collective-permute-start.5 = (bf16[64,128]{1,0:T(8,128)(2,1)S(1)}, bf16[64,128]{1,0:T(8,128)(2,1)S(1)}, u32[]{:S(2)}, u32[]{:S(2)}) collective-permute-start(bf16[64,128]{1,0:T(8,128)(2,1)S(1)} %collective-permute-done.3), channel_id=1, source_target_pairs={{0,28},{4,0},{8,4},{12,8},{16,12},{20,16},{24,20},{28,24},{1,29},{... | collective-permute-start | bytes 49160 | tf_op jit(solution)/shard_map/ppermute | solution.py:43
  29.5 6.4 %collective-permute-start.6 = (bf16[64,128]{1,0:T(8,128)(2,1)S(1)}, bf16[64,128]{1,0:T(8,128)(2,1)S(1)}, u32[]{:S(2)}, u32[]{:S(2)}) collective-permute-start(bf16[64,128]{1,0:T(8,128)(2,1)S(1)} %collective-permute-done.4), channel_id=1, source_target_pairs={{0,4},{4,8},{8,12},{12,16},{16,20},{20,24},{24,28},{28,0},{1,5},{5... | collective-permute-start | bytes 49160 | tf_op jit(solution)/shard_map/ppermute | solution.py:38
  36.9 40.3 %reduce-scatter.13.cloned.1.call-start = ((), (), s32[]{:S(2)}) async-start(), calls=%async_computation.8 | async-start | bytes 327680
  44.3 10.2 %copy-start.1 = (bf16[128,256]{1,0:T(8,128)(2,1)S(1)}, bf16[128,256]{1,0:T(8,128)(2,1)}, u32[]{:S(2)}) copy-start(bf16[128,256]{1,0:T(8,128)(2,1)} %param.6) | copy-start | bytes 196612
  56.5 21.7 %copy-start = (f32[256,128]{1,0:T(8,128)S(1)}, f32[256,128]{1,0:T(8,128)}, u32[]{:S(2)}) copy-start(f32[256,128]{1,0:T(8,128)} %param.4) | copy-start | bytes 393220
  56.5 87.3 %reduce-scatter.11.cloned.1.call-start = ((), (), s32[]{:S(2)}) async-start(), calls=%async_computation.7 | async-start | bytes 327680 | tf_op jit(solution)/shard_map/reduce_scatter | solution.py:54
  77.2 1.0 copy-start.2
  100.6 6.5 %collective-permute-start.7 = (bf16[64,128]{1,0:T(8,128)(2,1)S(1)}, bf16[64,128]{1,0:T(8,128)(2,1)S(1)}, u32[]{:S(2)}, u32[]{:S(2)}) collective-permute-start(bf16[64,128]{1,0:T(8,128)(2,1)S(1)} %get-tuple-element.6), channel_id=1, source_target_pairs={{0,4},{4,8},{8,12},{12,16},{16,20},{20,24},{24,28},{28,0},{1,5},{5... | collective-permute-start | bytes 49160 | tf_op jit(solution)/shard_map/ppermute | solution.py:38
  100.6 6.4 %collective-permute-start.8 = (bf16[64,128]{1,0:T(8,128)(2,1)S(1)}, bf16[64,128]{1,0:T(8,128)(2,1)S(1)}, u32[]{:S(2)}, u32[]{:S(2)}) collective-permute-start(bf16[64,128]{1,0:T(8,128)(2,1)S(1)} %get-tuple-element.6), channel_id=1, source_target_pairs={{0,28},{4,0},{8,4},{12,8},{16,12},{20,16},{24,20},{28,24},{1,29},{... | collective-permute-start | bytes 49160 | tf_op jit(solution)/shard_map/ppermute | solution.py:43
  107.1 6.4 %collective-permute-start.9 = (bf16[64,128]{1,0:T(8,128)(2,1)S(1)}, bf16[64,128]{1,0:T(8,128)(2,1)S(1)}, u32[]{:S(2)}, u32[]{:S(2)}) collective-permute-start(bf16[64,128]{1,0:T(8,128)(2,1)S(1)} %collective-permute-done.7), channel_id=1, source_target_pairs={{0,4},{4,8},{8,12},{12,16},{16,20},{20,24},{24,28},{28,0},{1,5},{5... | collective-permute-start | bytes 49160 | tf_op jit(solution)/shard_map/ppermute | solution.py:38
  107.1 6.4 %collective-permute-start.10 = (bf16[64,128]{1,0:T(8,128)(2,1)S(1)}, bf16[64,128]{1,0:T(8,128)(2,1)S(1)}, u32[]{:S(2)}, u32[]{:S(2)}) collective-permute-start(bf16[64,128]{1,0:T(8,128)(2,1)S(1)} %collective-permute-done.8), channel_id=1, source_target_pairs={{0,28},{4,0},{8,4},{12,8},{16,12},{20,16},{24,20},{28,24},{1,29},{... | collective-permute-start | bytes 49160 | tf_op jit(solution)/shard_map/ppermute | solution.py:43
  113.5 6.4 %collective-permute-start.11 = (bf16[64,128]{1,0:T(8,128)(2,1)S(1)}, bf16[64,128]{1,0:T(8,128)(2,1)S(1)}, u32[]{:S(2)}, u32[]{:S(2)}) collective-permute-start(bf16[64,128]{1,0:T(8,128)(2,1)S(1)} %collective-permute-done.9), channel_id=1, source_target_pairs={{0,4},{4,8},{8,12},{12,16},{16,20},{20,24},{24,28},{28,0},{1,5},{5... | collective-permute-start | bytes 49160 | tf_op jit(solution)/shard_map/ppermute | solution.py:38
  113.5 6.4 %collective-permute-start.12 = (bf16[64,128]{1,0:T(8,128)(2,1)S(1)}, bf16[64,128]{1,0:T(8,128)(2,1)S(1)}, u32[]{:S(2)}, u32[]{:S(2)}) collective-permute-start(bf16[64,128]{1,0:T(8,128)(2,1)S(1)} %collective-permute-done.10), channel_id=1, source_target_pairs={{0,28},{4,0},{8,4},{12,8},{16,12},{20,16},{24,20},{28,24},{1,29},{... | collective-permute-start | bytes 49160 | tf_op jit(solution)/shard_map/ppermute | solution.py:43
  119.9 6.4 %collective-permute-start.13 = (bf16[64,128]{1,0:T(8,128)(2,1)S(1)}, bf16[64,128]{1,0:T(8,128)(2,1)S(1)}, u32[]{:S(2)}, u32[]{:S(2)}) collective-permute-start(bf16[64,128]{1,0:T(8,128)(2,1)S(1)} %collective-permute-done.11), channel_id=1, source_target_pairs={{0,4},{4,8},{8,12},{12,16},{16,20},{20,24},{24,28},{28,0},{1,5},{5... | collective-permute-start | bytes 49160 | tf_op jit(solution)/shard_map/ppermute | solution.py:38
  127.3 39.1 %reduce-scatter.15.cloned.1.call-start = ((), (), s32[]{:S(2)}) async-start(), calls=%async_computation.9 | async-start | bytes 327680
Sparse Core Ops, SparseCore 0:
  37.0 17.4 reduce-scatter.8
  57.1 20.0 reduce-scatter.12
  127.4 16.3 reduce-scatter.10
  146.3 20.0 reduce-scatter.14
